TPU v7x, 128 devices: a whole 4x4x4 slice. The times are simulated.
128 devices in a mesh: tm: 16 (over z, y_lo, core), head: 8 (over y_hi, x).
Axes of the slice: x: 4, y: 4 (y_hi: 2, y_lo: 2; y = y_hi * 2 + y_lo), z: 4, core: 2. Of those that a mesh axis runs over, the one named last changes fastest.
Arguments:
- queries: bfloat16 [16384, 768], P(('tm', 'head')), may hold values from -64 to 64
- keys: bfloat16 [16384, 768], P(('tm', 'head')), may hold values from -4 to 4
- values: bfloat16 [16384, 768], P(('tm', 'head')), may hold values from -6 to 6
- grad_out: bfloat16 [16384, 768], P(('tm', 'head')), may hold values from -6 to 6
- frame_counts: int32 [4], replicated, may hold values from 1 to 8192, 16384 in all
Outputs:
- attended: bfloat16 [16384, 768], P(('tm', 'head'))
- grad_queries: bfloat16 [16384, 768], P(('tm', 'head'))
- grad_keys: bfloat16 [16384, 768], P(('tm', 'head'))
- grad_values: bfloat16 [16384, 768], P(('tm', 'head'))
All inputs are finite; a program needn't handle non-finite values.
Results may differ from a plain program's by a relative error of at most 0.029.
Values may be sent and summed in bfloat16 or wider, within the bound.
No kernel may reach another device: no remote copies, remote signals or barrier semaphores. Data moves between devices by JAX's collectives and lax.ppermute only.
A program may use at most 64 MiB of HBM per device.

v0:
```python
import math

import jax
import jax.numpy as jnp
from jax import lax
from jax.sharding import PartitionSpec as P

HEADS = 8
DH = 96


def segment_of(index, bounds):
    return jnp.sum((index[:, None] >= bounds[None, :]).astype(jnp.int32), axis=1)


def block_rows(unit, total_rows):
    count = total_rows // unit
    factor = max(1, min(count, 2048 // unit))
    while count % factor != 0:
        factor = factor - 1
    return unit * factor


def block_scores(query3, key3, seg_rows, seg_cols, scale):
    scores = jnp.einsum("qhd,khd->hqk", query3, key3, preferred_element_type=jnp.float32) * scale
    visible = (seg_rows[:, None] == seg_cols[None, :])[None, :, :]
    return (scores, visible)


def grad_terms(query3, grad3, log_total, delta, key3, value3, seg_rows, seg_cols, scale):
    scores, visible = block_scores(query3, key3, seg_rows, seg_cols, scale)
    weights = jnp.where(visible, jnp.exp(scores - log_total[:, :, None]), 0.0)
    weights_low = weights.astype(jnp.bfloat16)
    dprod = jnp.einsum("qhd,khd->hqk", grad3, value3, preferred_element_type=jnp.float32)
    dscore = (weights * (dprod - delta[:, :, None])).astype(jnp.bfloat16)
    return (weights_low, dscore)


def body(queries, keys, values, grad_out, frame_counts):
    heads_here = HEADS // lax.axis_size("head")
    scale = 1.0 / math.sqrt(DH)
    own_q, own_k, own_v, own_g = (
        lax.all_to_all(queries, "head", split_axis=1, concat_axis=0, tiled=True),
        lax.all_to_all(keys, "head", split_axis=1, concat_axis=0, tiled=True),
        lax.all_to_all(values, "head", split_axis=1, concat_axis=0, tiled=True),
        lax.all_to_all(grad_out, "head", split_axis=1, concat_axis=0, tiled=True),
    )
    rows = own_q.shape[0]
    all_k, all_v = (
        lax.all_gather(own_k, "tm", axis=0, tiled=True),
        lax.all_gather(own_v, "tm", axis=0, tiled=True),
    )
    nkeys = all_k.shape[0]
    bounds = jnp.cumsum(frame_counts)[:-1]
    offset = lax.axis_index("tm") * rows
    seg_own = segment_of(offset + jnp.arange(rows, dtype=jnp.int32), bounds)
    seg_keys = segment_of(jnp.arange(nkeys, dtype=jnp.int32), bounds)
    query3 = own_q.reshape(rows, heads_here, DH)
    grad3 = own_g.reshape(rows, heads_here, DH)
    kblock = block_rows(rows, nkeys)
    nblocks = nkeys // kblock
    key_blocks = all_k.reshape(nblocks, kblock, heads_here, DH)
    value_blocks = all_v.reshape(nblocks, kblock, heads_here, DH)
    seg_blocks = seg_keys.reshape(nblocks, kblock)
    blocks = (key_blocks, value_blocks, seg_blocks)

    def forward_step(carry, block):
        running_max, running_sum, out_acc = carry
        key3, value3, seg_cols = block
        scores, visible = block_scores(query3, key3, seg_own, seg_cols, scale)
        new_max = jnp.maximum(running_max, jnp.max(jnp.where(visible, scores, -1e30), axis=2))
        factor = jnp.exp(running_max - new_max)
        terms = jnp.where(visible, jnp.exp(scores - new_max[:, :, None]), 0.0)
        running_sum = running_sum * factor + jnp.sum(terms, axis=2)
        product = jnp.einsum(
            "hqk,khd->qhd", terms.astype(jnp.bfloat16), value3, preferred_element_type=jnp.float32
        )
        out_acc = out_acc * factor.T[:, :, None] + product
        return ((new_max, running_sum, out_acc), None)

    start_max = jnp.full((heads_here, rows), -1e30, jnp.float32)
    start_sum = jnp.zeros((heads_here, rows), jnp.float32)
    start_acc = jnp.zeros((rows, heads_here, DH), jnp.float32)
    (top, total, out_acc), unused = lax.scan(
        forward_step, (start_max, start_sum, start_acc), blocks
    )
    log_total = top + jnp.log(total)
    attended = (out_acc / total.T[:, :, None]).astype(jnp.bfloat16)
    delta = jnp.sum(grad3.astype(jnp.float32) * attended.astype(jnp.float32), axis=2).T
    zeros_q = jnp.zeros((rows, heads_here, DH), jnp.float32)

    def full_step(carry, block):
        key3, value3, seg_cols = block
        weights_low, dscore = grad_terms(
            query3, grad3, log_total, delta, key3, value3, seg_own, seg_cols, scale
        )
        carry = carry + jnp.einsum("hqk,khd->qhd", dscore, key3, preferred_element_type=jnp.float32)
        key_term = jnp.einsum("hqk,qhd->khd", dscore, query3, preferred_element_type=jnp.float32)
        value_term = jnp.einsum(
            "hqk,qhd->khd", weights_low, grad3, preferred_element_type=jnp.float32
        )
        return (carry, (key_term, value_term))

    dq_acc, (key_terms, value_terms) = lax.scan(full_step, zeros_q, blocks)
    key_terms = key_terms.reshape(nkeys, heads_here * DH)
    value_terms = value_terms.reshape(nkeys, heads_here * DH)
    dk_sum, dv_sum = (
        lax.psum_scatter(
            key_terms.astype(jnp.bfloat16), "tm", scatter_dimension=0, tiled=True
        ).astype(jnp.float32),
        lax.psum_scatter(
            value_terms.astype(jnp.bfloat16), "tm", scatter_dimension=0, tiled=True
        ).astype(jnp.float32),
    )
    grad_k = (scale * dk_sum).astype(jnp.bfloat16)
    grad_v = dv_sum.astype(jnp.bfloat16)
    grad_q = (scale * dq_acc).reshape(rows, heads_here * DH).astype(jnp.bfloat16)
    attended_flat = attended.reshape(rows, heads_here * DH)
    return (
        lax.all_to_all(attended_flat, "head", split_axis=0, concat_axis=1, tiled=True),
        lax.all_to_all(grad_q, "head", split_axis=0, concat_axis=1, tiled=True),
        lax.all_to_all(grad_k, "head", split_axis=0, concat_axis=1, tiled=True),
        lax.all_to_all(grad_v, "head", split_axis=0, concat_axis=1, tiled=True),
    )


def solution(mesh):
    placed = (
        P(("tm", "head"), None),
        P(("tm", "head"), None),
        P(("tm", "head"), None),
        P(("tm", "head"), None),
        P(),
    )
    return jax.shard_map(
        body,
        mesh=mesh,
        in_specs=placed,
        out_specs=(
            P(("tm", "head"), None),
            P(("tm", "head"), None),
            P(("tm", "head"), None),
            P(("tm", "head"), None),
        ),
        check_vma=False,
    )
```

profile of v0, /device:TPU:0, one launch (start us, length us, event | category | flops | bytes accessed | tf_op | source)
XLA Modules:
  0.0 433.8 jit_solution(16039583602134568563)
XLA Ops:
  8.3 15.3 %all_to_all.143 = bf16[128,8,96]{0,2,1:T(8,128)(2,1)S(1)} all-to-all(bf16[128,8,96]{0,2,1:T(8,128)(2,1)S(1)} %bitcast.268), channel_id=1, replica_groups=mesh['tm'=16,'head'=8] {'head'}, dimensions={1} | all-to-all | bytes 393216 | tf_op jit(solution)/shard_map/all_to_all | solution.py:44
  25.4 11.0 %all_to_all.144 = bf16[128,8,96]{0,2,1:T(8,128)(2,1)S(1)} all-to-all(bf16[128,8,96]{0,2,1:T(8,128)(2,1)S(1)} %bitcast.269), channel_id=1, replica_groups=mesh['tm'=16,'head'=8] {'head'}, dimensions={1} | all-to-all | bytes 393216 | tf_op jit(solution)/shard_map/all_to_all | solution.py:45
  45.8 4.9 %all-to-all-done.1 = bf16[128,8,96]{0,2,1:T(8,128)(2,1)S(1)} async-done(((bf16[128,8,96]{0,2,1:T(8,128)(2,1)}), bf16[128,8,96]{0,2,1:T(8,128)(2,1)S(1)}, u32[]{:S(2)}, u32[]{:S(2)}) %all-to-all-start.1) | async-done | bytes 196640 | tf_op jit(solution)/shard_map/all_to_all | solution.py:43
  54.5 8.0 %all-to-all-done.4 = bf16[128,8,96]{0,2,1:T(8,128)(2,1)S(1)} async-done(((bf16[128,8,96]{0,2,1:T(8,128)(2,1)}), bf16[128,8,96]{0,2,1:T(8,128)(2,1)S(1)}, u32[]{:S(2)}, u32[]{:S(2)}) %all-to-all-start.4) | async-done | bytes 196640 | tf_op jit(solution)/shard_map/all_to_all | solution.py:46
  62.7 4.1 copy.106
  68.6 28.3 %all-gather.5.cloned.1.call-done = bf16[16384,96]{0,1:T(8,128)(2,1)} async-done(((bf16[1024,96]{0,1:T(8,128)(2,1)}), bf16[16384,96]{0,1:T(8,128)(2,1)}) %all-gather.5.cloned.1.call-update) | async-done | bytes 3145744 | tf_op jit(solution)/shard_map/all_gather | solution.py:51
  96.8 4.1 copy.107
  104.3 65.9 %while.30 = (s32[]{:T(128)}, f32[1,1024]{1,0:T(1,128)S(1)}, f32[1,1024]{1,0:T(1,128)S(1)}, f32[1024,1,96]{0,2,1:T(8,128)}, s32[1024]{0:T(1024)S(1)}, /*index=5*/...) while((s32[]{:T(128)}, f32[1,1024]{1,0:T(1,128)S(1)}, ...), condition=%wide.region_6.7_spmd.clone, body=%wide.region_3.6_spmd.clone.sunk | while | flops 834966528 | bytes 30200004 | solution.py:84
  171.9 93.9 %while.31 = (s32[]{:T(128)}, f32[1024,1,96]{0,2,1:T(8,128)}, bf16[8,2048,1,96]{1,3,2,0:T(8,128)(2,1)}, bf16[8,2048,1,96]{1,3,2,0:T(8,128)(2,1)}, bf16[8,2048,1,9...) while((s32[]{:T(128)}, f32[1024,1,96]{0,2,1:T(8,128)}, ...), condition=%wide.region_9.10_spmd.clone, body=%wide.region_8.9_spmd.clone.sunk | while | flops 2038628352 | bytes 45273316 | solution.py:104
  176.8 3.7 fusion.102
  188.6 3.7 fusion.102
  212.0 3.7 fusion.102
  223.7 3.7 fusion.102
  235.5 3.7 fusion.102
  247.2 3.7 fusion.102
  259.0 3.7 fusion.102
  265.8 4.1 copy.111
  273.6 6.5 %all-to-all-start.3 = ((bf16[8,128,96]{1,2,0:T(8,128)(2,1)}), bf16[8,128,96]{1,2,0:T(8,128)(2,1)S(1)}, u32[]{:S(2)}, u32[]{:S(2)}) async-start(bf16[8,128,96]{1,2,0:T(8,128)(2,1)} %copy.88), calls=%async_computation.3 | async-start | bytes 393216 | tf_op jit(solution)/shard_map/all_to_all | solution.py:120
  280.8 7.7 %all-to-all-done.3 = bf16[8,128,96]{1,2,0:T(8,128)(2,1)S(1)} async-done(((bf16[8,128,96]{1,2,0:T(8,128)(2,1)}), bf16[8,128,96]{1,2,0:T(8,128)(2,1)S(1)}, u32[]{:S(2)}, u32[]{:S(2)}) %all-to-all-start.3) | async-done | bytes 196640 | tf_op jit(solution)/shard_map/all_to_all | solution.py:120
  291.9 47.6 %reduce-scatter.5.cloned.1.call-done = bf16[1024,96]{0,1:T(8,128)(2,1)} async-done(((bf16[16384,96]{0,1:T(8,128)(2,1)}), bf16[1024,96]{0,1:T(8,128)(2,1)}) %reduce-scatter.5.cloned.1.call-update) | async-done | bytes 196624 | tf_op jit(solution)/shard_map/reduce_scatter | solution.py:111
  341.2 7.1 %all-to-all-start.7 = ((bf16[8,128,96]{1,2,0:T(8,128)(2,1)}), bf16[8,128,96]{1,2,0:T(8,128)(2,1)S(1)}, u32[]{:S(2)}, u32[]{:S(2)}) async-start(bf16[8,128,96]{1,2,0:T(8,128)(2,1)} %copy_bitcast_fusion.2), calls=%async_computation.9 | async-start | bytes 393216 | tf_op jit(solution)/shard_map/all_to_all | solution.py:123
  348.3 61.6 %reduce-scatter.3.cloned.1.call-done = bf16[1024,96]{0,1:T(8,128)(2,1)} async-done(((bf16[16384,96]{0,1:T(8,128)(2,1)}), bf16[1024,96]{0,1:T(8,128)(2,1)}) %reduce-scatter.3.cloned.1.call-update) | async-done | bytes 196624 | tf_op jit(solution)/shard_map/reduce_scatter | solution.py:108
  411.5 6.5 %all-to-all-start.6 = ((bf16[8,128,96]{1,2,0:T(8,128)(2,1)}), bf16[8,128,96]{1,2,0:T(8,128)(2,1)S(1)}, u32[]{:S(2)}, u32[]{:S(2)}) async-start(bf16[8,128,96]{1,2,0:T(8,128)(2,1)} %copy_bitcast_fusion.3), calls=%async_computation.7 | async-start | bytes 393216 | tf_op jit(solution)/shard_map/all_to_all | solution.py:122
  420.4 6.0 %all-to-all-done.6 = bf16[8,128,96]{1,2,0:T(8,128)(2,1)S(1)} async-done(((bf16[8,128,96]{1,2,0:T(8,128)(2,1)}), bf16[8,128,96]{1,2,0:T(8,128)(2,1)S(1)}, u32[]{:S(2)}, u32[]{:S(2)}) %all-to-all-start.6) | async-done | bytes 196640 | tf_op jit(solution)/shard_map/all_to_all | solution.py:122
  (217 shorter events, 170.2 us)
Async XLA Ops:
  7.2 55.5 %all-gather.3.cloned.1.call-start = ((), (), s32[]{:S(2)}) async-start(), calls=%async_computation.10 | async-start | bytes 3342336 | tf_op jit(solution)/shard_map/all_gather | solution.py:50
  24.3 72.5 %all-gather.5.cloned.1.call-start = ((), (), s32[]{:S(2)}) async-start(), calls=%async_computation.11 | async-start | bytes 3342336 | tf_op jit(solution)/shard_map/all_gather | solution.py:51
  38.9 11.9 %all-to-all-start.1 = ((bf16[128,8,96]{0,2,1:T(8,128)(2,1)}), bf16[128,8,96]{0,2,1:T(8,128)(2,1)S(1)}, u32[]{:S(2)}, u32[]{:S(2)}) async-start(bf16[128,8,96]{0,2,1:T(8,128)(2,1)} %bitcast.4), calls=%async_computation.1 | async-start | bytes 393216 | tf_op jit(solution)/shard_map/all_to_all | solution.py:43
  50.7 11.8 %all-to-all-start.4 = ((bf16[128,8,96]{0,2,1:T(8,128)(2,1)}), bf16[128,8,96]{0,2,1:T(8,128)(2,1)S(1)}, u32[]{:S(2)}, u32[]{:S(2)}) async-start(bf16[128,8,96]{0,2,1:T(8,128)(2,1)} %bitcast.11), calls=%async_computation.4 | async-start | bytes 393216 | tf_op jit(solution)/shard_map/all_to_all | solution.py:46
  54.1 285.4 %reduce-scatter.5.cloned.1.call-start = ((), (), s32[]{:S(2)}) async-start(), calls=%async_computation.13 | async-start | bytes 3342336 | tf_op jit(solution)/shard_map/reduce_scatter | solution.py:111
  176.8 3.7 copy-start
  188.6 3.8 copy-start
  200.3 3.7 copy-start
  212.0 3.7 copy-start
  216.6 2.2 copy-start.1
  223.7 3.8 copy-start
  228.4 2.2 copy-start.1
  235.5 3.8 copy-start
  240.1 2.2 copy-start.1
  247.2 3.8 copy-start
  251.9 2.2 copy-start.1
  259.0 3.8 copy-start
  265.8 4.2 copy-start.3
  269.9 10.1 %copy-start.2 = (f32[1024,1,96]{0,2,1:T(8,128)S(1)}, f32[1024,1,96]{0,2,1:T(8,128)}, u32[]{:S(2)}) copy-start(f32[1024,1,96]{0,2,1:T(8,128)} %get-tuple-element.120) | copy-start | bytes 1179652
  269.9 139.9 %reduce-scatter.3.cloned.1.call-start = ((), (), s32[]{:S(2)}) async-start(), calls=%async_computation.12 | async-start | bytes 3342336 | tf_op jit(solution)/shard_map/reduce_scatter | solution.py:108
  273.6 14.9 %all-to-all-start.3 = ((bf16[8,128,96]{1,2,0:T(8,128)(2,1)}), bf16[8,128,96]{1,2,0:T(8,128)(2,1)S(1)}, u32[]{:S(2)}, u32[]{:S(2)}) async-start(bf16[8,128,96]{1,2,0:T(8,128)(2,1)} %copy.88), calls=%async_computation.3 | async-start | bytes 393216 | tf_op jit(solution)/shard_map/all_to_all | solution.py:120
  288.5 52.7 %all-to-all-start.5 = ((bf16[8,128,96]{1,2,0:T(8,128)(2,1)}), bf16[8,128,96]{1,2,0:T(8,128)(2,1)S(1)}, u32[]{:S(2)}, u32[]{:S(2)}) async-start(bf16[8,128,96]{1,2,0:T(8,128)(2,1)} %copy.93), calls=%async_computation.5 | async-start | bytes 393216 | tf_op jit(solution)/shard_map/all_to_all | solution.py:121
  341.2 70.3 %all-to-all-start.7 = ((bf16[8,128,96]{1,2,0:T(8,128)(2,1)}), bf16[8,128,96]{1,2,0:T(8,128)(2,1)S(1)}, u32[]{:S(2)}, u32[]{:S(2)}) async-start(bf16[8,128,96]{1,2,0:T(8,128)(2,1)} %copy_bitcast_fusion.2), calls=%async_computation.9 | async-start | bytes 393216 | tf_op jit(solution)/shard_map/all_to_all | solution.py:123
  411.5 14.9 %all-to-all-start.6 = ((bf16[8,128,96]{1,2,0:T(8,128)(2,1)}), bf16[8,128,96]{1,2,0:T(8,128)(2,1)S(1)}, u32[]{:S(2)}, u32[]{:S(2)}) async-start(bf16[8,128,96]{1,2,0:T(8,128)(2,1)} %copy_bitcast_fusion.3), calls=%async_computation.7 | async-start | bytes 393216 | tf_op jit(solution)/shard_map/all_to_all | solution.py:122
  (20 other events, 31.3 us)
Sparse Core Ops, SparseCore 0:
  24.4 34.5 all-gather.2
  61.3 35.4 all-gather.4
  270.0 69.4 reduce-scatter.4
  341.8 67.9 reduce-scatter.2
where the time goes:
time: 436 us; the launch traced here: 434 us
  waiting for transfers between devices  164 us (38%)
  matrix products  123 us (28%)
  local copies, waits for them, and re-layouts  54.4 us (12%)
  starting transfers between devices  30.4 us (7%)
  blocking collectives  26.3 us (6%)
  other arithmetic  20.8 us (5%)
  between operations  13.9 us (3%)
    reduce_scatter x1, waiting for transfers between devices, body(): lax.psum_scatter(key_terms.astype(jnp.bfloat16), 'tm', scatter_dimension=...  61.6 us
    reduce_scatter x1, waiting for transfers between devices, body(): lax.psum_scatter(value_terms.astype(jnp.bfloat16), 'tm', scatter_dimensio...  47.6 us
    dot_general x8, matrix products, grad_terms(): jnp.einsum('qhd,khd->hqk', grad3, value3, preferred_element_type=jnp.floa...  29.9 us
    unnamed x20, local copies, waits for them, and re-layouts  29.2 us
    all_gather x1, waiting for transfers between devices, body(): lax.all_gather(own_v, 'tm', axis=0, tiled=True)  28.3 us
    dot_general x8, matrix products, forward_step(): jnp.einsum('hqk,khd->qhd', terms.astype(jnp.bfloat16), value3, preferred_...  23.3 us
    dot_general x16, matrix products, block_scores(): jnp.einsum('qhd,khd->hqk', query3, key3, preferred_element_type=jnp.float32)  23.2 us
    dot_general x8, matrix products, full_step(): jnp.einsum('hqk,qhd->khd', weights_low, grad3, preferred_element_type=jnp...  22.1 us
  transfers between devices with their start and end apart: 10, of which 7 were waited for; matrix products, arithmetic and copies ran while one was open for 5% of the time, Pallas kernels for 0%

commit v1 on v0

v1 whole, which is shorter than its diff:
```python
import math

import jax
import jax.numpy as jnp
from jax import lax
from jax.experimental import pallas as pl
from jax.experimental.pallas import tpu as pltpu
from jax.sharding import PartitionSpec as P

HEADS = 8
DH = 96
KBLOCK = 512
NEG = -1e30


def segment_of(index, bounds):
    return jnp.sum((index[:, None] >= bounds[None, :]).astype(jnp.int32), axis=1)


def fwd_kernel(rng_ref, segq_ref, q_ref, k_ref, v_ref, g_ref, segk_ref,
               att_ref, lse_ref, delta_ref, m_sc, l_sc, acc_sc, *, scale):
    j = pl.program_id(0)
    lo = rng_ref[0]
    hi = rng_ref[1]

    @pl.when(j == 0)
    def _():
        m_sc[...] = jnp.full(m_sc.shape, NEG, jnp.float32)
        l_sc[...] = jnp.zeros(l_sc.shape, jnp.float32)
        acc_sc[...] = jnp.zeros(acc_sc.shape, jnp.float32)

    @pl.when(lo + j <= hi)
    def _():
        s = lax.dot_general(q_ref[...], k_ref[...], (((1,), (1,)), ((), ())),
                            preferred_element_type=jnp.float32) * scale
        vis = segq_ref[...] == segk_ref[...]
        m_prev = m_sc[...]
        m_new = jnp.maximum(m_prev, jnp.max(jnp.where(vis, s, NEG), axis=1, keepdims=True))
        alpha = jnp.exp(m_prev - m_new)
        p = jnp.where(vis, jnp.exp(s - m_new), 0.0)
        l_sc[...] = l_sc[...] * alpha + jnp.sum(p, axis=1, keepdims=True)
        acc_sc[...] = acc_sc[...] * alpha + jnp.dot(
            p.astype(jnp.bfloat16), v_ref[...], preferred_element_type=jnp.float32)
        m_sc[...] = m_new

    @pl.when(j == pl.num_programs(0) - 1)
    def _():
        total = l_sc[...]
        att = (acc_sc[...] / total).astype(jnp.bfloat16)
        att_ref[...] = att
        lse_ref[...] = m_sc[...] + jnp.log(total)
        delta_ref[...] = jnp.sum(g_ref[...].astype(jnp.float32) * att.astype(jnp.float32),
                                 axis=1, keepdims=True)


def bwd_kernel(rng_ref, segq_ref, q_ref, g_ref, lse_ref, delta_ref, k_ref, v_ref, segk_ref,
               dq_ref, dk_ref, dv_ref, dq_sc, *, scale):
    j = pl.program_id(0)
    lo = rng_ref[0]
    hi = rng_ref[1]
    active = jnp.logical_and(j >= lo, j <= hi)

    @pl.when(j == 0)
    def _():
        dq_sc[...] = jnp.zeros(dq_sc.shape, jnp.float32)

    @pl.when(active)
    def _():
        q = q_ref[...]
        g = g_ref[...]
        k = k_ref[...]
        s = lax.dot_general(q, k, (((1,), (1,)), ((), ())),
                            preferred_element_type=jnp.float32) * scale
        vis = segq_ref[...] == segk_ref[...]
        w = jnp.where(vis, jnp.exp(s - lse_ref[...]), 0.0)
        dp = lax.dot_general(g, v_ref[...], (((1,), (1,)), ((), ())),
                             preferred_element_type=jnp.float32)
        ds = (w * (dp - delta_ref[...])).astype(jnp.bfloat16)
        dq_sc[...] += jnp.dot(ds, k, preferred_element_type=jnp.float32)
        dk_ref[...] = lax.dot_general(ds, q, (((0,), (0,)), ((), ())),
                                      preferred_element_type=jnp.float32).astype(jnp.bfloat16)
        dv_ref[...] = lax.dot_general(w.astype(jnp.bfloat16), g, (((0,), (0,)), ((), ())),
                                      preferred_element_type=jnp.float32).astype(jnp.bfloat16)

    @pl.when(jnp.logical_not(active))
    def _():
        dk_ref[...] = jnp.zeros(dk_ref.shape, dk_ref.dtype)
        dv_ref[...] = jnp.zeros(dv_ref.shape, dv_ref.dtype)

    @pl.when(j == pl.num_programs(0) - 1)
    def _():
        dq_ref[...] = (scale * dq_sc[...]).astype(jnp.bfloat16)


def attention_head(rng, segq, segk, q, k, v, g, scale):
    rows = q.shape[0]
    nkeys = k.shape[0]
    nk = nkeys // KBLOCK
    full = lambda j, r: (0, 0)
    kmap_f = lambda j, r: (jnp.minimum(r[0] + j, r[1]), 0)
    skmap_f = lambda j, r: (0, jnp.minimum(r[0] + j, r[1]))
    fwd = pl.pallas_call(
        lambda *refs: fwd_kernel(*refs, scale=scale),
        grid_spec=pltpu.PrefetchScalarGridSpec(
            num_scalar_prefetch=1,
            grid=(nk,),
            in_specs=[
                pl.BlockSpec((rows, 1), full),
                pl.BlockSpec((rows, DH), full),
                pl.BlockSpec((KBLOCK, DH), kmap_f),
                pl.BlockSpec((KBLOCK, DH), kmap_f),
                pl.BlockSpec((rows, DH), full),
                pl.BlockSpec((1, KBLOCK), skmap_f),
            ],
            out_specs=[
                pl.BlockSpec((rows, DH), full),
                pl.BlockSpec((rows, 1), full),
                pl.BlockSpec((rows, 1), full),
            ],
            scratch_shapes=[
                pltpu.VMEM((rows, 1), jnp.float32),
                pltpu.VMEM((rows, 1), jnp.float32),
                pltpu.VMEM((rows, DH), jnp.float32),
            ],
        ),
        out_shape=[
            jax.ShapeDtypeStruct((rows, DH), jnp.bfloat16),
            jax.ShapeDtypeStruct((rows, 1), jnp.float32),
            jax.ShapeDtypeStruct((rows, 1), jnp.float32),
        ],
        compiler_params=pltpu.CompilerParams(dimension_semantics=("arbitrary",)),
    )
    att, lse, delta = fwd(rng, segq, q, k, v, g, segk)

    kmap_b = lambda j, r: (jnp.minimum(jnp.maximum(j, r[0]), r[1]), 0)
    skmap_b = lambda j, r: (0, jnp.minimum(jnp.maximum(j, r[0]), r[1]))
    omap = lambda j, r: (j, 0)
    bwd = pl.pallas_call(
        lambda *refs: bwd_kernel(*refs, scale=scale),
        grid_spec=pltpu.PrefetchScalarGridSpec(
            num_scalar_prefetch=1,
            grid=(nk,),
            in_specs=[
                pl.BlockSpec((rows, 1), full),
                pl.BlockSpec((rows, DH), full),
                pl.BlockSpec((rows, DH), full),
                pl.BlockSpec((rows, 1), full),
                pl.BlockSpec((rows, 1), full),
                pl.BlockSpec((KBLOCK, DH), kmap_b),
                pl.BlockSpec((KBLOCK, DH), kmap_b),
                pl.BlockSpec((1, KBLOCK), skmap_b),
            ],
            out_specs=[
                pl.BlockSpec((rows, DH), full),
                pl.BlockSpec((KBLOCK, DH), omap),
                pl.BlockSpec((KBLOCK, DH), omap),
            ],
            scratch_shapes=[pltpu.VMEM((rows, DH), jnp.float32)],
        ),
        out_shape=[
            jax.ShapeDtypeStruct((rows, DH), jnp.bfloat16),
            jax.ShapeDtypeStruct((nkeys, DH), jnp.bfloat16),
            jax.ShapeDtypeStruct((nkeys, DH), jnp.bfloat16),
        ],
        compiler_params=pltpu.CompilerParams(dimension_semantics=("arbitrary",)),
    )
    dq, dk, dv = bwd(rng, segq, q, g, lse, delta, k, v, segk)
    return att, dq, dk, dv


def body(queries, keys, values, grad_out, frame_counts):
    heads_here = HEADS // lax.axis_size("head")
    scale = 1.0 / math.sqrt(DH)
    own_q, own_k, own_v, own_g = (
        lax.all_to_all(queries, "head", split_axis=1, concat_axis=0, tiled=True),
        lax.all_to_all(keys, "head", split_axis=1, concat_axis=0, tiled=True),
        lax.all_to_all(values, "head", split_axis=1, concat_axis=0, tiled=True),
        lax.all_to_all(grad_out, "head", split_axis=1, concat_axis=0, tiled=True),
    )
    rows = own_q.shape[0]
    all_k, all_v = (
        lax.all_gather(own_k, "tm", axis=0, tiled=True),
        lax.all_gather(own_v, "tm", axis=0, tiled=True),
    )
    nkeys = all_k.shape[0]
    nk = nkeys // KBLOCK
    bounds = jnp.cumsum(frame_counts)[:-1].astype(jnp.int32)
    offset = lax.axis_index("tm") * rows
    seg_own = segment_of(offset + jnp.arange(rows, dtype=jnp.int32), bounds)
    seg_keys = segment_of(jnp.arange(nkeys, dtype=jnp.int32), bounds)
    starts = jnp.concatenate([jnp.zeros((1,), jnp.int32), bounds])
    ends = jnp.concatenate([bounds, jnp.full((1,), nkeys, jnp.int32)])
    kstart = starts[seg_own[0]]
    kend = ends[seg_own[rows - 1]]
    rng = jnp.clip(jnp.stack([kstart // KBLOCK, (kend - 1) // KBLOCK]), 0, nk - 1).astype(jnp.int32)
    segq = seg_own.reshape(rows, 1)
    segk = seg_keys.reshape(1, nkeys)

    atts, dqs, dks, dvs = [], [], [], []
    for h in range(heads_here):
        cols = slice(h * DH, (h + 1) * DH)
        att, dq, dk, dv = attention_head(
            rng, segq, segk, own_q[:, cols], all_k[:, cols], all_v[:, cols], own_g[:, cols], scale)
        atts.append(att)
        dqs.append(dq)
        dks.append(dk)
        dvs.append(dv)
    attended_flat = jnp.concatenate(atts, axis=1)
    grad_q = jnp.concatenate(dqs, axis=1)
    key_terms = jnp.concatenate(dks, axis=1)
    value_terms = jnp.concatenate(dvs, axis=1)
    dk_sum, dv_sum = (
        lax.psum_scatter(key_terms, "tm", scatter_dimension=0, tiled=True).astype(jnp.float32),
        lax.psum_scatter(value_terms, "tm", scatter_dimension=0, tiled=True).astype(jnp.float32),
    )
    grad_k = (scale * dk_sum).astype(jnp.bfloat16)
    grad_v = dv_sum.astype(jnp.bfloat16)
    return (
        lax.all_to_all(attended_flat, "head", split_axis=0, concat_axis=1, tiled=True),
        lax.all_to_all(grad_q, "head", split_axis=0, concat_axis=1, tiled=True),
        lax.all_to_all(grad_k, "head", split_axis=0, concat_axis=1, tiled=True),
        lax.all_to_all(grad_v, "head", split_axis=0, concat_axis=1, tiled=True),
    )


def solution(mesh):
    placed = (
        P(("tm", "head"), None),
        P(("tm", "head"), None),
        P(("tm", "head"), None),
        P(("tm", "head"), None),
        P(),
    )
    return jax.shard_map(
        body,
        mesh=mesh,
        in_specs=placed,
        out_specs=(
            P(("tm", "head"), None),
            P(("tm", "head"), None),
            P(("tm", "head"), None),
            P(("tm", "head"), None),
        ),
        check_vma=False,
    )
```

time: 436 us -> 365 us (0.84)
  matrix products: 123 us -> 0 us
  waiting for transfers between devices: 164 us -> 219 us
  Pallas kernels: 0 us -> 44.8 us
  local copies, waits for them, and re-layouts: 54.4 us -> 19.7 us
  other arithmetic: 20.8 us -> 3.52 us
  between operations: 13.9 us -> 21 us
    dot_general x56 -> x0, matrix products: 123 us -> none  [the longest x8 29.9 us: grad_terms(): jnp.einsum('qhd,khd->hqk', grad3, value3, preferred_element_type=jnp.floa...]
    reduce_scatter x2, waiting for transfers between devices: 109 us -> 170 us  [the longest x1 106 us: body(): lax.psum_scatter(key_terms, 'tm', scatter_dimension=0, tiled=True)]
    pallas_call x0 -> x2, Pallas kernels: none -> 44.8 us  [the longest x1 26.3 us: attention_head(): dq, dk, dv = bwd(rng, segq, q, g, lse, delta, k, v, segk)]
    unnamed x20 -> x12, local copies, waits for them, and re-layouts: 29.2 us -> 9.32 us
    reduce_sum x9 -> x0, other arithmetic: 17.6 us -> none  [the longest x8 15.9 us: forward_step(): running_sum = running_sum * factor + jnp.sum(terms, axis=2)]
    dynamic_slice x16 -> x2, local copies, waits for them, and re-layouts: 13.6 us -> 1.17 us  [the longest x1 0.59 us: body(): kend = ends[seg_own[rows - 1]]]
    while x72 -> x0, local copies, waits for them, and re-layouts: 6.21 us -> none
    all_to_all x1, waiting for transfers between devices: 5.96 us -> 0.01 us  [body(): lax.all_to_all(grad_k, 'head', split_axis=0, concat_axis=1, tiled=True)]
  transfers between devices with their start and end apart: 10 -> 10, of which waited for: 7 -> 6; matrix products, arithmetic and copies ran while one was open for 5% -> 5% of each run, Pallas kernels for 0% -> 0%
where the time goes in v1:
time: 365 us; the launch traced here: 367 us
  waiting for transfers between devices  219 us (60%)
  Pallas kernels  44.8 us (12%)
  starting transfers between devices  32.7 us (9%)
  blocking collectives  26.2 us (7%)
  between operations  21 us (6%)
  local copies, waits for them, and re-layouts  19.7 us (5%)
    reduce_scatter x1, waiting for transfers between devices, body(): lax.psum_scatter(key_terms, 'tm', scatter_dimension=0, tiled=True)  106 us
    reduce_scatter x1, waiting for transfers between devices, body(): lax.psum_scatter(value_terms, 'tm', scatter_dimension=0, tiled=True)  64.1 us
    all_gather x1, waiting for transfers between devices, body(): lax.all_gather(own_v, 'tm', axis=0, tiled=True)  29.6 us
    pallas_call x1, Pallas kernels, attention_head(): dq, dk, dv = bwd(rng, segq, q, g, lse, delta, k, v, segk)  26.3 us
    pallas_call x1, Pallas kernels, attention_head(): att, lse, delta = fwd(rng, segq, q, k, v, g, segk)  18.4 us
    all_to_all x1, blocking collectives, body(): lax.all_to_all(keys, 'head', split_axis=1, concat_axis=0, tiled=True)  15.3 us
    all_to_all x1, blocking collectives, body(): lax.all_to_all(values, 'head', split_axis=1, concat_axis=0, tiled=True)  11 us
    unnamed x12, local copies, waits for them, and re-layouts  9.32 us
  transfers between devices with their start and end apart: 10, of which 6 were waited for; matrix products, arithmetic and copies ran while one was open for 5% of the time, Pallas kernels for 0%

profile of v1, /device:TPU:0, one launch (start us, length us, event | category | flops | bytes accessed | tf_op | source)
XLA Modules:
  0.0 366.8 jit_solution(720762167123648019)
XLA Ops:
  7.2 1.1 copy.37
  8.3 15.3 %all_to_all.152 = bf16[128,8,96]{0,2,1:T(8,128)(2,1)S(1)} all-to-all(bf16[128,8,96]{0,2,1:T(8,128)(2,1)S(1)} %bitcast.54), channel_id=1, replica_groups=mesh['tm'=16,'head'=8] {'head'}, dimensions={1} | all-to-all | bytes 393216 | tf_op jit(solution)/shard_map/all_to_all | solution.py:176
  24.5 1.1 copy.39
  25.6 11.0 %all_to_all.153 = bf16[128,8,96]{0,2,1:T(8,128)(2,1)S(1)} all-to-all(bf16[128,8,96]{0,2,1:T(8,128)(2,1)S(1)} %bitcast.55), channel_id=1, replica_groups=mesh['tm'=16,'head'=8] {'head'}, dimensions={1} | all-to-all | bytes 393216 | tf_op jit(solution)/shard_map/all_to_all | solution.py:177
  37.5 1.8 copy.35
  39.2 3.4 all-to-all-start
  52.5 1.8 copy.41
  54.3 7.1 %all-to-all-start.3 = ((bf16[128,8,96]{0,2,1:T(8,128)(2,1)}), bf16[128,8,96]{0,2,1:T(8,128)(2,1)S(1)}, u32[]{:S(2)}, u32[]{:S(2)}) async-start(bf16[128,8,96]{0,2,1:T(8,128)(2,1)} %bitcast.18), calls=%async_computation.3 | async-start | bytes 393216 | tf_op jit(solution)/shard_map/all_to_all | solution.py:178
  62.1 1.0 copy.43.refs_1_
  63.1 0.9 convert_reduce_fusion
  64.9 5.0 %all-to-all-done.3 = bf16[128,8,96]{0,2,1:T(8,128)(2,1)S(1)} async-done(((bf16[128,8,96]{0,2,1:T(8,128)(2,1)}), bf16[128,8,96]{0,2,1:T(8,128)(2,1)S(1)}, u32[]{:S(2)}, u32[]{:S(2)}) %all-to-all-start.3) | async-done | bytes 196640 | tf_op jit(solution)/shard_map/all_to_all | solution.py:178
  70.7 29.6 %all-gather.5.cloned.1.call-done.refs_4_.refs_7_ = bf16[16384,96]{1,0:T(8,128)(2,1)} async-done(((bf16[1024,96]{1,0:T(8,128)(2,1)}), bf16[16384,96]{1,0:T(8,128)(2,1)}) %all-gather.5.cloned.1.call-update) | async-done | bytes 3145744 | tf_op jit(solution)/shard_map/all_gather | solution.py:183
  100.3 18.4 %shard_map.84 = (bf16[1024,96]{1,0:T(8,128)(2,1)}, f32[1024,1]{1,0:T(8,128)}, f32[1024,1]{1,0:T(8,128)}) custom-call(s32[2]{0:T(128)} %add_clamp_fusion.refs_0_, s32[1024,1]{1,0:T(8,128)} %copy.43.refs_1_, bf16[1024,96]{1,0:T(8,128)(2,1)} %bitcast.39, bf16[16384,96]{1,0:T(8,128)(2,1)} %all-gather.3.cloned.1.call-done.refs_3_.refs_6_, ...), custom_call_target="tpu_custom_call" | custom-call | tf_op jit(solution)/shard_map/pallas_call | solution.py:133
  118.7 26.3 %shard_map.85 = (bf16[1024,96]{1,0:T(8,128)(2,1)}, bf16[16384,96]{1,0:T(8,128)(2,1)}, bf16[16384,96]{1,0:T(8,128)(2,1)}) custom-call(s32[2]{0:T(128)} %add_clamp_fusion.refs_0_, s32[1024,1]{1,0:T(8,128)} %copy.43.refs_1_, bf16[1024,96]{1,0:T(8,128)(2,1)} %bitcast.40, bf16[1024,96]{1,0:T(8,128)(2,1)} %bitcast.42, f32[1024,1]{1,0:T(8,128)} %get-tuple-element.11.refs_4_, ...), custom_call_target="tpu_custom_call" | custom-call | tf_op jit(solution)/shard_map/pallas_call | solution.py:167
  146.8 6.4 %all-to-all-start.4 = ((bf16[8,128,96]{1,2,0:T(8,128)(2,1)}), bf16[8,128,96]{1,2,0:T(8,128)(2,1)S(1)}, u32[]{:S(2)}, u32[]{:S(2)}) async-start(bf16[8,128,96]{1,2,0:T(8,128)(2,1)} %copy.44), calls=%async_computation.4 | async-start | bytes 393216 | tf_op jit(solution)/shard_map/all_to_all | solution.py:219
  154.1 7.6 %all-to-all-done.4 = bf16[8,128,96]{1,2,0:T(8,128)(2,1)S(1)} async-done(((bf16[8,128,96]{1,2,0:T(8,128)(2,1)}), bf16[8,128,96]{1,2,0:T(8,128)(2,1)S(1)}, u32[]{:S(2)}, u32[]{:S(2)}) %all-to-all-start.4) | async-done | bytes 196640 | tf_op jit(solution)/shard_map/all_to_all | solution.py:219
  161.7 3.4 all-to-all-start.5
  165.1 106.0 %reduce-scatter.3.cloned.1.call-done = bf16[1024,96]{1,0:T(8,128)(2,1)} async-done(((bf16[16384,96]{1,0:T(8,128)(2,1)}), bf16[1024,96]{1,0:T(8,128)(2,1)}) %reduce-scatter.3.cloned.1.call-update) | async-done | bytes 196624 | tf_op jit(solution)/shard_map/reduce_scatter | solution.py:213
  271.2 1.0 multiply_convert_fusion
  273.0 6.3 %all-to-all-start.6 = ((bf16[8,128,96]{1,2,0:T(8,128)(2,1)}), bf16[8,128,96]{1,2,0:T(8,128)(2,1)S(1)}, u32[]{:S(2)}, u32[]{:S(2)}) async-start(bf16[8,128,96]{1,2,0:T(8,128)(2,1)} %copy.47), calls=%async_computation.7 | async-start | bytes 393216 | tf_op jit(solution)/shard_map/all_to_all | solution.py:221
  279.3 64.1 %reduce-scatter.5.cloned.1.call-done = bf16[1024,96]{1,0:T(8,128)(2,1)} async-done(((bf16[16384,96]{1,0:T(8,128)(2,1)}), bf16[1024,96]{1,0:T(8,128)(2,1)}) %reduce-scatter.5.cloned.1.call-update) | async-done | bytes 196624 | tf_op jit(solution)/shard_map/reduce_scatter | solution.py:214
  343.4 1.8 copy.48
  345.2 5.8 %all-to-all-start.7 = ((bf16[8,128,96]{1,2,0:T(8,128)(2,1)}), bf16[8,128,96]{1,2,0:T(8,128)(2,1)S(1)}, u32[]{:S(2)}, u32[]{:S(2)}) async-start(bf16[8,128,96]{1,2,0:T(8,128)(2,1)} %copy.48), calls=%async_computation.9 | async-start | bytes 393216 | tf_op jit(solution)/shard_map/all_to_all | solution.py:222
  353.5 6.0 %all-to-all-done.7 = bf16[8,128,96]{1,2,0:T(8,128)(2,1)S(1)} async-done(((bf16[8,128,96]{1,2,0:T(8,128)(2,1)}), bf16[8,128,96]{1,2,0:T(8,128)(2,1)S(1)}, u32[]{:S(2)}, u32[]{:S(2)}) %all-to-all-start.7) | async-done | bytes 196640 | tf_op jit(solution)/shard_map/all_to_all | solution.py:222
  (36 shorter events, 13.6 us)
Async XLA Ops:
  7.2 63.6 %all-gather.3.cloned.1.call-start = ((), (), s32[]{:S(2)}) async-start(), calls=%async_computation.10 | async-start | bytes 4456448 | tf_op jit(solution)/shard_map/all_gather | solution.py:182
  24.5 75.8 %all-gather.5.cloned.1.call-start = ((), (), s32[]{:S(2)}) async-start(), calls=%async_computation.11 | async-start | bytes 4456448 | tf_op jit(solution)/shard_map/all_gather | solution.py:183
  39.2 15.1 %all-to-all-start = ((bf16[128,8,96]{0,2,1:T(8,128)(2,1)}), bf16[128,8,96]{0,2,1:T(8,128)(2,1)S(1)}, u32[]{:S(2)}, u32[]{:S(2)}) async-start(bf16[128,8,96]{0,2,1:T(8,128)(2,1)} %bitcast.9), calls=%async_computation | async-start | bytes 393216 | tf_op jit(solution)/shard_map/all_to_all | solution.py:175
  54.3 15.6 %all-to-all-start.3 = ((bf16[128,8,96]{0,2,1:T(8,128)(2,1)}), bf16[128,8,96]{0,2,1:T(8,128)(2,1)S(1)}, u32[]{:S(2)}, u32[]{:S(2)}) async-start(bf16[128,8,96]{0,2,1:T(8,128)(2,1)} %bitcast.18), calls=%async_computation.3 | async-start | bytes 393216 | tf_op jit(solution)/shard_map/all_to_all | solution.py:178
  61.4 209.7 %reduce-scatter.3.cloned.1.call-start = ((), (), s32[]{:S(2)}) async-start(), calls=%async_computation.12 | async-start | bytes 4456448 | tf_op jit(solution)/shard_map/reduce_scatter | solution.py:213
  145.1 0.9 copy-start.1
  145.1 8.2 %copy-start = (bf16[1024,96]{1,0:T(8,128)(2,1)S(1)}, bf16[1024,96]{1,0:T(8,128)(2,1)}, u32[]{:S(2)}) copy-start(bf16[1024,96]{1,0:T(8,128)(2,1)} %get-tuple-element.13) | copy-start | bytes 589828
  145.1 198.3 %reduce-scatter.5.cloned.1.call-start = ((), (), s32[]{:S(2)}) async-start(), calls=%async_computation.13 | async-start | bytes 4456448 | tf_op jit(solution)/shard_map/reduce_scatter | solution.py:214
  146.8 14.9 %all-to-all-start.4 = ((bf16[8,128,96]{1,2,0:T(8,128)(2,1)}), bf16[8,128,96]{1,2,0:T(8,128)(2,1)S(1)}, u32[]{:S(2)}, u32[]{:S(2)}) async-start(bf16[8,128,96]{1,2,0:T(8,128)(2,1)} %copy.44), calls=%async_computation.4 | async-start | bytes 393216 | tf_op jit(solution)/shard_map/all_to_all | solution.py:219
  161.7 111.3 %all-to-all-start.5 = ((bf16[8,128,96]{1,2,0:T(8,128)(2,1)}), bf16[8,128,96]{1,2,0:T(8,128)(2,1)S(1)}, u32[]{:S(2)}, u32[]{:S(2)}) async-start(bf16[8,128,96]{1,2,0:T(8,128)(2,1)} %copy.46), calls=%async_computation.5 | async-start | bytes 393216 | tf_op jit(solution)/shard_map/all_to_all | solution.py:220
  273.0 72.2 %all-to-all-start.6 = ((bf16[8,128,96]{1,2,0:T(8,128)(2,1)}), bf16[8,128,96]{1,2,0:T(8,128)(2,1)S(1)}, u32[]{:S(2)}, u32[]{:S(2)}) async-start(bf16[8,128,96]{1,2,0:T(8,128)(2,1)} %copy.47), calls=%async_computation.7 | async-start | bytes 393216 | tf_op jit(solution)/shard_map/all_to_all | solution.py:221
  345.2 14.3 %all-to-all-start.7 = ((bf16[8,128,96]{1,2,0:T(8,128)(2,1)}), bf16[8,128,96]{1,2,0:T(8,128)(2,1)S(1)}, u32[]{:S(2)}, u32[]{:S(2)}) async-start(bf16[8,128,96]{1,2,0:T(8,128)(2,1)} %copy.48), calls=%async_computation.9 | async-start | bytes 393216 | tf_op jit(solution)/shard_map/all_to_all | solution.py:222
Sparse Core Ops, SparseCore 0:
  24.6 36.4 all-gather.2
  62.8 37.4 all-gather.4
  145.2 125.9 reduce-scatter.2
  273.4 69.9 reduce-scatter.4

commit v2 on v1

v2 whole, which is shorter than its diff:
```python
import math

import jax
import jax.numpy as jnp
from jax import lax
from jax.experimental import pallas as pl
from jax.experimental.pallas import tpu as pltpu
from jax.sharding import PartitionSpec as P

HEADS = 8
DH = 96
KBLOCK = 512
NEG = -1e30


def segment_of(index, bounds):
    return jnp.sum((index[:, None] >= bounds[None, :]).astype(jnp.int32), axis=1)


def fwd_kernel(rng_ref, segq_ref, q_ref, k_ref, v_ref, g_ref, segk_ref,
               att_ref, lse_ref, delta_ref, m_sc, l_sc, acc_sc, *, scale):
    j = pl.program_id(0)
    lo = rng_ref[0]
    hi = rng_ref[1]

    @pl.when(j == 0)
    def _():
        m_sc[...] = jnp.full(m_sc.shape, NEG, jnp.float32)
        l_sc[...] = jnp.zeros(l_sc.shape, jnp.float32)
        acc_sc[...] = jnp.zeros(acc_sc.shape, jnp.float32)

    @pl.when(lo + j <= hi)
    def _():
        s = lax.dot_general(q_ref[...], k_ref[...], (((1,), (1,)), ((), ())),
                            preferred_element_type=jnp.float32) * scale
        vis = segq_ref[...] == segk_ref[...]
        m_prev = m_sc[...]
        m_new = jnp.maximum(m_prev, jnp.max(jnp.where(vis, s, NEG), axis=1, keepdims=True))
        alpha = jnp.exp(m_prev - m_new)
        p = jnp.where(vis, jnp.exp(s - m_new), 0.0)
        l_sc[...] = l_sc[...] * alpha + jnp.sum(p, axis=1, keepdims=True)
        acc_sc[...] = acc_sc[...] * alpha + jnp.dot(
            p.astype(jnp.bfloat16), v_ref[...], preferred_element_type=jnp.float32)
        m_sc[...] = m_new

    @pl.when(j == pl.num_programs(0) - 1)
    def _():
        total = l_sc[...]
        att = (acc_sc[...] / total).astype(jnp.bfloat16)
        att_ref[...] = att
        lse_ref[...] = m_sc[...] + jnp.log(total)
        delta_ref[...] = jnp.sum(g_ref[...].astype(jnp.float32) * att.astype(jnp.float32),
                                 axis=1, keepdims=True)


def dq_kernel(rng_ref, segq_ref, q_ref, g_ref, lse_ref, delta_ref, k_ref, v_ref, segk_ref,
              dq_ref, dq_sc, *, scale):
    j = pl.program_id(0)
    lo = rng_ref[0]
    hi = rng_ref[1]

    @pl.when(j == 0)
    def _():
        dq_sc[...] = jnp.zeros(dq_sc.shape, jnp.float32)

    @pl.when(lo + j <= hi)
    def _():
        k = k_ref[...]
        s = lax.dot_general(q_ref[...], k, (((1,), (1,)), ((), ())),
                            preferred_element_type=jnp.float32) * scale
        vis = segq_ref[...] == segk_ref[...]
        w = jnp.where(vis, jnp.exp(s - lse_ref[...]), 0.0)
        dp = lax.dot_general(g_ref[...], v_ref[...], (((1,), (1,)), ((), ())),
                             preferred_element_type=jnp.float32)
        ds = (w * (dp - delta_ref[...])).astype(jnp.bfloat16)
        dq_sc[...] += jnp.dot(ds, k, preferred_element_type=jnp.float32)

    @pl.when(j == pl.num_programs(0) - 1)
    def _():
        dq_ref[...] = (scale * dq_sc[...]).astype(jnp.bfloat16)


def dkv_kernel(rng_ref, segk_own_ref, k_ref, v_ref, q_ref, g_ref, lse_ref, delta_ref, segq_ref,
               dk_ref, dv_ref, dk_sc, dv_sc, *, scale):
    i = pl.program_id(0)
    lo = rng_ref[0]
    hi = rng_ref[1]

    @pl.when(i == 0)
    def _():
        dk_sc[...] = jnp.zeros(dk_sc.shape, jnp.float32)
        dv_sc[...] = jnp.zeros(dv_sc.shape, jnp.float32)

    @pl.when(lo + i <= hi)
    def _():
        q = q_ref[...]
        g = g_ref[...]
        st = lax.dot_general(k_ref[...], q, (((1,), (1,)), ((), ())),
                             preferred_element_type=jnp.float32) * scale
        vis = segk_own_ref[...] == segq_ref[...]
        wt = jnp.where(vis, jnp.exp(st - lse_ref[...]), 0.0)
        dpt = lax.dot_general(v_ref[...], g, (((1,), (1,)), ((), ())),
                              preferred_element_type=jnp.float32)
        dst = (wt * (dpt - delta_ref[...])).astype(jnp.bfloat16)
        dk_sc[...] += jnp.dot(dst, q, preferred_element_type=jnp.float32)
        dv_sc[...] += jnp.dot(wt.astype(jnp.bfloat16), g, preferred_element_type=jnp.float32)

    @pl.when(i == pl.num_programs(0) - 1)
    def _():
        dk_ref[...] = (scale * dk_sc[...]).astype(jnp.bfloat16)
        dv_ref[...] = dv_sc[...].astype(jnp.bfloat16)


def block_call(kernel, rng, fixed, streamed, outs, scratch, nblocks):
    full = lambda j, r: (0, 0)
    rowmap = lambda j, r: (jnp.minimum(r[0] + j, r[1]), 0)
    colmap = lambda j, r: (0, jnp.minimum(r[0] + j, r[1]))
    in_specs = [pl.BlockSpec(a.shape, full) for a in fixed]
    for a, blk, by_row in streamed:
        in_specs.append(pl.BlockSpec(blk, rowmap if by_row else colmap))
    return pl.pallas_call(
        kernel,
        grid_spec=pltpu.PrefetchScalarGridSpec(
            num_scalar_prefetch=1,
            grid=(nblocks,),
            in_specs=in_specs,
            out_specs=[pl.BlockSpec(o.shape, full) for o in outs],
            scratch_shapes=scratch,
        ),
        out_shape=outs,
        compiler_params=pltpu.CompilerParams(dimension_semantics=("arbitrary",)),
    )(rng, *fixed, *[a for a, _, _ in streamed])


def body(queries, keys, values, grad_out, frame_counts):
    n_head = lax.axis_size("head")
    heads_here = HEADS // n_head
    scale = 1.0 / math.sqrt(DH)
    rows_in = queries.shape[0]
    stacked = jnp.stack(
        [a.reshape(rows_in, HEADS, DH) for a in (queries, keys, values, grad_out)], axis=2
    ).reshape(rows_in, HEADS * 4 * DH)
    mine = lax.all_to_all(stacked, "head", split_axis=1, concat_axis=0, tiled=True)
    rows = mine.shape[0]
    mine = mine.reshape(rows, heads_here, 4, DH)
    nkeys = rows * lax.axis_size("tm")
    nk = nkeys // KBLOCK
    bounds = jnp.cumsum(frame_counts)[:-1].astype(jnp.int32)
    offset = lax.axis_index("tm") * rows
    seg_own = segment_of(offset + jnp.arange(rows, dtype=jnp.int32), bounds)
    seg_keys = segment_of(jnp.arange(nkeys, dtype=jnp.int32), bounds)
    starts = jnp.concatenate([jnp.zeros((1,), jnp.int32), bounds])
    ends = jnp.concatenate([bounds, jnp.full((1,), nkeys, jnp.int32)])
    kstart = starts[seg_own[0]]
    kend = ends[seg_own[rows - 1]]
    rng = jnp.clip(jnp.stack([kstart // KBLOCK, (kend - 1) // KBLOCK]), 0, nk - 1).astype(jnp.int32)
    segq = seg_own.reshape(rows, 1)
    segk = seg_keys.reshape(1, nkeys)
    f32 = jnp.float32
    bf16 = jnp.bfloat16

    outs_a, outs_b = [], []
    for h in range(heads_here):
        own_q, own_k, own_v, own_g = (mine[:, h, c, :] for c in range(4))
        all_k = lax.all_gather(own_k, "tm", axis=0, tiled=True)
        all_v = lax.all_gather(own_v, "tm", axis=0, tiled=True)
        all_q = lax.all_gather(own_q, "tm", axis=0, tiled=True)
        all_g = lax.all_gather(own_g, "tm", axis=0, tiled=True)
        att, lse, delta = fwd_call(rng, segq, own_q, all_k, all_v, own_g, segk, scale, nk)
        (dq,) = block_call(
            lambda *refs: dq_kernel(*refs, scale=scale), rng,
            [segq, own_q, own_g, lse, delta],
            [(all_k, (KBLOCK, DH), True), (all_v, (KBLOCK, DH), True), (segk, (1, KBLOCK), False)],
            [jax.ShapeDtypeStruct((rows, DH), bf16)],
            [pltpu.VMEM((rows, DH), f32)],
            nk,
        )
        all_lse = lax.all_gather(lse.reshape(1, rows), "tm", axis=1, tiled=True)
        all_delta = lax.all_gather(delta.reshape(1, rows), "tm", axis=1, tiled=True)
        dk, dv = block_call(
            lambda *refs: dkv_kernel(*refs, scale=scale), rng,
            [segq, own_k, own_v],
            [(all_q, (KBLOCK, DH), True), (all_g, (KBLOCK, DH), True),
             (all_lse, (1, KBLOCK), False), (all_delta, (1, KBLOCK), False),
             (segk, (1, KBLOCK), False)],
            [jax.ShapeDtypeStruct((rows, DH), bf16), jax.ShapeDtypeStruct((rows, DH), bf16)],
            [pltpu.VMEM((rows, DH), f32), pltpu.VMEM((rows, DH), f32)],
            nk,
        )
        outs_a.append(jnp.stack([att, dq], axis=1))
        outs_b.append(jnp.stack([dk, dv], axis=1))

    def send_back(parts):
        packed = jnp.stack(parts, axis=1).reshape(rows, heads_here * 2 * DH)
        back = lax.all_to_all(packed, "head", split_axis=0, concat_axis=1, tiled=True)
        back = back.reshape(rows_in, HEADS, 2, DH)
        return back[:, :, 0, :].reshape(rows_in, HEADS * DH), back[:, :, 1, :].reshape(rows_in, HEADS * DH)

    attended, grad_q = send_back(outs_a)
    grad_k, grad_v = send_back(outs_b)
    return attended, grad_q, grad_k, grad_v


def fwd_call(rng, segq, q, k, v, g, segk, scale, nk):
    rows = q.shape[0]
    f32 = jnp.float32
    full = lambda j, r: (0, 0)
    kmap = lambda j, r: (jnp.minimum(r[0] + j, r[1]), 0)
    skmap = lambda j, r: (0, jnp.minimum(r[0] + j, r[1]))
    return pl.pallas_call(
        lambda *refs: fwd_kernel(*refs, scale=scale),
        grid_spec=pltpu.PrefetchScalarGridSpec(
            num_scalar_prefetch=1,
            grid=(nk,),
            in_specs=[
                pl.BlockSpec((rows, 1), full),
                pl.BlockSpec((rows, DH), full),
                pl.BlockSpec((KBLOCK, DH), kmap),
                pl.BlockSpec((KBLOCK, DH), kmap),
                pl.BlockSpec((rows, DH), full),
                pl.BlockSpec((1, KBLOCK), skmap),
            ],
            out_specs=[
                pl.BlockSpec((rows, DH), full),
                pl.BlockSpec((rows, 1), full),
                pl.BlockSpec((rows, 1), full),
            ],
            scratch_shapes=[
                pltpu.VMEM((rows, 1), f32),
                pltpu.VMEM((rows, 1), f32),
                pltpu.VMEM((rows, DH), f32),
            ],
        ),
        out_shape=[
            jax.ShapeDtypeStruct((rows, DH), jnp.bfloat16),
            jax.ShapeDtypeStruct((rows, 1), f32),
            jax.ShapeDtypeStruct((rows, 1), f32),
        ],
        compiler_params=pltpu.CompilerParams(dimension_semantics=("arbitrary",)),
    )(rng, segq, q, k, v, g, segk)


def solution(mesh):
    placed = (
        P(("tm", "head"), None),
        P(("tm", "head"), None),
        P(("tm", "head"), None),
        P(("tm", "head"), None),
        P(),
    )
    return jax.shard_map(
        body,
        mesh=mesh,
        in_specs=placed,
        out_specs=(
            P(("tm", "head"), None),
            P(("tm", "head"), None),
            P(("tm", "head"), None),
            P(("tm", "head"), None),
        ),
        check_vma=False,
    )
```

time: 365 us -> 442 us (1.21)
  the two profiles are of different devices: /device:TPU:0 before, /device:TPU:33 now
where the time goes in v2:
time: 442 us; the launch traced here: 449 us
  blocking collectives  203 us (46%)
  Pallas kernels  109 us (25%)
  waiting for transfers between devices  67.6 us (15%)
  between operations  21.1 us (5%)
  local copies, waits for them, and re-layouts  17 us (4%)
  starting transfers between devices  16 us (4%)
  other arithmetic  14.8 us (3%)
    all_gather x1, blocking collectives, body(): all_delta = lax.all_gather(delta.reshape(1, rows), 'tm', axis=1, tiled=True)  95.6 us
    all_gather x1, blocking collectives, body(): all_lse = lax.all_gather(lse.reshape(1, rows), 'tm', axis=1, tiled=True)  87.8 us
    pallas_call x2, Pallas kernels, block_call(): pl.pallas_call(kernel, grid_spec=pltpu.PrefetchScalarGridSpec(num_scalar_...  66.9 us
    pallas_call x1, Pallas kernels, fwd_call(): pl.pallas_call(lambda *refs: fwd_kernel(*refs, scale=scale), grid_spec=pl...  42 us
    all_gather x1, waiting for transfers between devices, body(): all_v = lax.all_gather(own_v, 'tm', axis=0, tiled=True)  38.9 us
    all_gather x1, waiting for transfers between devices, body(): all_k = lax.all_gather(own_k, 'tm', axis=0, tiled=True)  21.9 us
    all_to_all x1, blocking collectives, body(): lax.all_to_all(stacked, 'head', split_axis=1, concat_axis=0, tiled=True)  20 us
    all_to_all x2, starting transfers between devices, send_back(): lax.all_to_all(packed, 'head', split_axis=0, concat_axis=1, tiled=True)  15.8 us
  transfers between devices with their start and end apart: 6, of which 3 were waited for; matrix products, arithmetic and copies ran while one was open for 5% of the time, Pallas kernels for 24%

profile of v2, /device:TPU:33, one launch (start us, length us, event | category | flops | bytes accessed | tf_op | source)
XLA Modules:
  0.0 448.7 jit_solution(4384796311485897620)
XLA Ops:
  7.2 1.1 copy.54
  8.3 1.1 copy.53
  9.4 1.1 copy.52
  10.5 1.1 copy.51
  11.8 20.0 %all_to_all.48 = bf16[128,8,384]{0,2,1:T(8,128)(2,1)S(1)} all-to-all(bf16[128,8,384]{0,2,1:T(8,128)(2,1)S(1)} %bitcast.63), channel_id=1, replica_groups=mesh['tm'=16,'head'=8] {'head'}, dimensions={1} | all-to-all | bytes 1572864 | tf_op jit(solution)/shard_map/all_to_all | solution.py:143
  32.7 0.8 copy.73
  34.5 0.8 copy.72
  35.4 0.9 copy.75
  45.6 1.0 copy.61.refs_1_
  47.2 0.9 convert_reduce_fusion
  48.2 21.9 %all-gather.11.cloned.1.call-done = bf16[16384,1,1,96]{3,0,2,1:T(8,128)(2,1)} async-done(((bf16[1024,1,1,96]{3,0,2,1:T(8,128)(2,1)}), bf16[16384,1,1,96]{3,0,2,1:T(8,128)(2,1)}) %all-gather.11.cloned.1.call-update) | async-done | bytes 3145744 | tf_op jit(solution)/shard_map/all_gather | solution.py:165
  70.1 38.9 %all-gather.13.cloned.1.call-done = bf16[16384,1,1,96]{3,0,2,1:T(8,128)(2,1)} async-done(((bf16[1024,1,1,96]{3,0,2,1:T(8,128)(2,1)}), bf16[16384,1,1,96]{3,0,2,1:T(8,128)(2,1)}) %all-gather.13.cloned.1.call-update) | async-done | bytes 3145744 | tf_op jit(solution)/shard_map/all_gather | solution.py:166
  109.0 42.0 %shard_map.84 = (bf16[1024,96]{1,0:T(8,128)(2,1)}, f32[1024,1]{1,0:T(8,128)}, f32[1024,1]{1,0:T(8,128)}) custom-call(s32[2]{0:T(128)} %add_clamp_fusion.refs_0_, s32[1024,1]{1,0:T(8,128)} %copy.61.refs_1_, bf16[1024,96]{1,0:T(8,128)(2,1)} %bitcast.59, bf16[16384,96]{1,0:T(8,128)(2,1)} %bitcast.53, bf16[16384,96]{1,0:T(8,128)(2,1)} %bitcast.55, ...), custom_call_target="tpu_custom_call" | custom-call | tf_op jit(solution)/shard_map/pallas_call | solution.py:210
  151.0 31.4 %shard_map.85 = bf16[1024,96]{1,0:T(8,128)(2,1)} custom-call(s32[2]{0:T(128)} %add_clamp_fusion.refs_0_, s32[1024,1]{1,0:T(8,128)} %copy.61.refs_1_, bf16[1024,96]{1,0:T(8,128)(2,1)} %bitcast.60, bf16[1024,96]{1,0:T(8,128)(2,1)} %bitcast.62, f32[1024,1]{1,0:T(8,128)} %get-tuple-element.10.refs_4_, f32[1024,1]{1,0:T(8,128)} %get-tuple-element.11.refs_5_, ...), custom_call_target="tpu_custom_call" | custom-call | tf_op jit(solution)/shard_map/pallas_call | solution.py:121
  182.4 1.1 pad_maximum_fusion.1
  184.7 6.1 %all-to-all-start.1 = ((bf16[8,128,192]{1,2,0:T(8,128)(2,1)}), bf16[8,128,192]{1,2,0:T(8,128)(2,1)S(1)}, u32[]{:S(2)}, u32[]{:S(2)}) async-start(bf16[8,128,192]{1,2,0:T(8,128)(2,1)} %copy.64), calls=%async_computation.1 | async-start | bytes 786432 | tf_op jit(solution)/shard_map/all_to_all | solution.py:195
  190.8 87.8 %all-gather.4 = f32[16384,1]{1,0:T(8,128)} all-gather(f32[1024,1]{1,0:T(8,128)S(1)} %copy-done.1), channel_id=6, replica_groups=mesh['tm'=16,'head'=8] {'tm'}, dimensions={0}, use_global_device_ids=true | all-gather | bytes 69632 | tf_op jit(solution)/shard_map/all_gather | solution.py:178
  278.6 5.3 %reduce = f32[16384]{0:T(1024)} reduce(f32[16384,1]{1,0:T(8,128)} %all-gather.4, f32[]{:T(128)} %constant.47), dimensions={1}, to_apply=%all-gather.4.reduce_sub_computation | reduce | bytes 131076 | tf_op jit(solution)/shard_map/all_gather | solution.py:178
  283.9 95.6 %all-gather.5 = f32[16384,1]{1,0:T(8,128)} all-gather(f32[1024,1]{1,0:T(8,128)S(1)} %copy-done), channel_id=7, replica_groups=mesh['tm'=16,'head'=8] {'tm'}, dimensions={0}, use_global_device_ids=true | all-gather | bytes 69632 | tf_op jit(solution)/shard_map/all_gather | solution.py:179
  379.4 5.3 %reduce.1 = f32[16384]{0:T(1024)} reduce(f32[16384,1]{1,0:T(8,128)} %all-gather.5, f32[]{:T(128)} %constant.47), dimensions={1}, to_apply=%all-gather.5.reduce_sub_computation | reduce | bytes 131076 | tf_op jit(solution)/shard_map/all_gather | solution.py:179
  384.7 35.5 %shard_map.86 = (bf16[1024,96]{1,0:T(8,128)(2,1)}, bf16[1024,96]{1,0:T(8,128)(2,1)}) custom-call(s32[2]{0:T(128)} %add_clamp_fusion.refs_0_, s32[1024,1]{1,0:T(8,128)} %copy.61.refs_1_, bf16[1024,96]{1,0:T(8,128)(2,1)} %bitcast.65, bf16[1024,96]{1,0:T(8,128)(2,1)} %bitcast.66, bf16[16384,96]{1,0:T(8,128)(2,1)} %bitcast.57, bf16[16384,96]{1,0:T(8,128)(2,1)} %bitcast.58, ...), custom_call_target="tpu_custom_call" | custom-call | tf_op jit(solution)/shard_map/pallas_call | solution.py:121
  420.2 1.1 pad_maximum_fusion.2
  422.4 9.7 %all-to-all-start.2 = ((bf16[8,128,192]{1,2,0:T(8,128)(2,1)}), bf16[8,128,192]{1,2,0:T(8,128)(2,1)S(1)}, u32[]{:S(2)}, u32[]{:S(2)}) async-start(bf16[8,128,192]{1,2,0:T(8,128)(2,1)} %copy.67), calls=%async_computation.2 | async-start | bytes 786432 | tf_op jit(solution)/shard_map/all_to_all | solution.py:195
  433.8 6.7 %all-to-all-done.2 = bf16[8,128,192]{1,2,0:T(8,128)(2,1)S(1)} async-done(((bf16[8,128,192]{1,2,0:T(8,128)(2,1)}), bf16[8,128,192]{1,2,0:T(8,128)(2,1)S(1)}, u32[]{:S(2)}, u32[]{:S(2)}) %all-to-all-start.2) | async-done | bytes 393248 | tf_op jit(solution)/shard_map/all_to_all | solution.py:195
  (46 shorter events, 10.3 us)
Async XLA Ops:
  7.2 62.9 %all-gather.11.cloned.1.call-start = ((), (), s32[]{:S(2)}) async-start(), calls=%async_computation.3 | async-start | bytes 4456448 | tf_op jit(solution)/shard_map/all_gather | solution.py:165
  31.8 4.6 %copy-start.3 = (s32[4]{0:T(128)S(1)}, s32[4]{0:T(128)}, u32[]{:S(2)}) copy-start(s32[4]{0:T(128)} %param.9) | copy-start | bytes 52
  33.5 75.5 %all-gather.13.cloned.1.call-start = ((), (), s32[]{:S(2)}) async-start(), calls=%async_computation.4 | async-start | bytes 4456448 | tf_op jit(solution)/shard_map/all_gather | solution.py:166
  34.5 350.2 %all-gather.15.cloned.1.call-start = ((), (), s32[]{:S(2)}) async-start(), calls=%async_computation.5 | async-start | bytes 4456448 | tf_op jit(solution)/shard_map/all_gather | solution.py:167
  35.4 349.3 %all-gather.17.cloned.1.call-start = ((), (), s32[]{:S(2)}) async-start(), calls=%async_computation.6 | async-start | bytes 4456448 | tf_op jit(solution)/shard_map/all_gather | solution.py:168
  151.0 31.4 %copy-start.2 = (bf16[1024,96]{1,0:T(8,128)(2,1)S(1)}, bf16[1024,96]{1,0:T(8,128)(2,1)}, u32[]{:S(2)}) copy-start(bf16[1024,96]{1,0:T(8,128)(2,1)} %get-tuple-element.9) | copy-start | bytes 589828
  182.4 8.4 %copy-start.1 = (f32[1024,1]{1,0:T(8,128)S(1)}, f32[1024,1]{1,0:T(8,128)}, u32[]{:S(2)}) copy-start(f32[1024,1]{1,0:T(8,128)} %get-tuple-element.10.refs_4_) | copy-start | bytes 12292
  184.7 237.7 %all-to-all-start.1 = ((bf16[8,128,192]{1,2,0:T(8,128)(2,1)}), bf16[8,128,192]{1,2,0:T(8,128)(2,1)S(1)}, u32[]{:S(2)}, u32[]{:S(2)}) async-start(bf16[8,128,192]{1,2,0:T(8,128)(2,1)} %copy.64), calls=%async_computation.1 | async-start | bytes 786432 | tf_op jit(solution)/shard_map/all_to_all | solution.py:195
  278.6 5.3 %copy-start = (f32[1024,1]{1,0:T(8,128)S(1)}, f32[1024,1]{1,0:T(8,128)}, u32[]{:S(2)}) copy-start(f32[1024,1]{1,0:T(8,128)} %get-tuple-element.11.refs_5_) | copy-start | bytes 12292
  422.4 18.0 %all-to-all-start.2 = ((bf16[8,128,192]{1,2,0:T(8,128)(2,1)}), bf16[8,128,192]{1,2,0:T(8,128)(2,1)S(1)}, u32[]{:S(2)}, u32[]{:S(2)}) async-start(bf16[8,128,192]{1,2,0:T(8,128)(2,1)} %copy.67), calls=%async_computation.2 | async-start | bytes 786432 | tf_op jit(solution)/shard_map/all_to_all | solution.py:195
Sparse Core Ops, SparseCore 0:
  33.7 36.4 all-gather.10
  71.8 37.1 all-gather.12
  110.7 37.2 all-gather.14
  149.6 46.9 all-gather.16
